TPU v7x, 32 devices: a whole 2x2x4 slice. The times are simulated.
32 devices in a mesh: rows: 8 (over z, y), sub: 4 (over x, core).
Axes of the slice: x: 2, y: 2, z: 4, core: 2. Of those that a mesh axis runs over, the one named last changes fastest.
Arguments:
- held: float32 [512, 4, 128, 256], P('rows', 'sub'), may hold values from -256 to 256
- held_block: int32 [512, 4], P('rows', 'sub'), may hold values from 0 to 255, as said below
- held_count: int32 [8, 4], P('rows', 'sub'), may hold values from 0 to 64
Outputs:
- q_factor: float32 [256, 4, 128, 256], P('rows', 'sub')
- r_factor: float32 [256, 256], replicated
Inputs may be any that keep to these rules, and one draw needn't show every extreme that they name: `held_block`: for slots j < held_count of a device, the ids are block numbers of its column group; over all devices of a column group each block is held in exactly one such slot. Slots at or past held_count hold arbitrary ids and data. A device holds at most 8 blocks whose number b has b // 32 equal to any one given device index along rows, and some device reaches that.
All inputs are finite; a program needn't handle non-finite values.
Results may differ from a plain program's by a relative error of at most 0.0003.
Values sent between devices are 32-bit elements; how exact they have to be, the bound alone decides.
No kernel may reach another device: no remote copies, remote signals or barrier semaphores. Data moves between devices by JAX's collectives and lax.ppermute only.
A program may use at most 128 MiB of HBM per device.

v0:
```python
import jax
import jax.numpy as jnp
from jax import lax
from jax.sharding import PartitionSpec as P

BLK_DEV = 32


def factor(gram):
    lower = jnp.linalg.cholesky(gram)
    identity = jnp.eye(gram.shape[0], dtype=gram.dtype)
    inverse = lax.linalg.triangular_solve(lower, identity, left_side=True, lower=True)
    return (lower, inverse)


def gram_of(flattened, total):
    return (
        lax.dot_general(
            flattened,
            flattened,
            (((0,), (0,)), ((), ())),
            precision=lax.Precision.HIGHEST,
            preferred_element_type=jnp.float32,
        )
        / total
    )


def apply_inverse(flattened, inverse):
    return jnp.dot(
        flattened, inverse.T, precision=lax.Precision.HIGHEST, preferred_element_type=jnp.float32
    )


def reduce_gram(partial_value):
    return lax.psum(partial_value, ("rows", "sub"))


def per_device(held, held_block, held_count):
    capacity = held.shape[0]
    block_rows = held.shape[2]
    width = held.shape[3]
    devices_rows = lax.axis_size("rows")
    own_index = lax.axis_index("rows")
    per_slot = max(1, capacity // devices_rows)
    total = float(devices_rows * lax.axis_size("sub") * BLK_DEV * block_rows)
    blocks = held[:, 0]
    block_ids = held_block[:, 0]
    count = held_count[0, 0]
    slots = jnp.arange(capacity, dtype=jnp.int32)
    valid = slots < count
    destination = block_ids // BLK_DEV
    earlier = (
        (destination[:, None] == destination[None, :])
        & valid[None, :]
        & (slots[None, :] < slots[:, None])
    )
    rank_within = jnp.sum(earlier.astype(jnp.int32), axis=1)
    target = jnp.where(valid, destination * per_slot + rank_within, devices_rows * per_slot)
    labels_out = block_ids.astype(jnp.float32)
    outgoing = (
        jnp.zeros((devices_rows * per_slot, block_rows, width), jnp.float32)
        .at[target]
        .set(blocks, mode="drop")
    )
    labels = (
        jnp.full((devices_rows * per_slot,), -1.0, jnp.float32)
        .at[target]
        .set(labels_out, mode="drop")
    )
    arrived = lax.all_to_all(outgoing, "rows", split_axis=0, concat_axis=0, tiled=True)
    arrived_labels = lax.all_to_all(labels, "rows", split_axis=0, concat_axis=0, tiled=True)
    local = arrived_labels.astype(jnp.int32) - own_index * BLK_DEV
    place = jnp.where(arrived_labels >= 0.0, local, BLK_DEV)
    resident = (
        jnp.zeros((BLK_DEV, block_rows, width), jnp.float32).at[place].set(arrived, mode="drop")
    )
    flattened = resident.reshape(-1, width)
    partial_one = gram_of(flattened, total)
    lower_one, inverse_one = factor(reduce_gram(partial_one))
    first = apply_inverse(flattened, inverse_one)
    lower_two, inverse_two = factor(reduce_gram(gram_of(first, total)))
    second, lower_one, lower_two = (apply_inverse(first, inverse_two), lower_one, lower_two)
    result = second.reshape(BLK_DEV, block_rows, width)
    r_factor = jnp.dot(
        lower_two.T,
        lower_one.T,
        precision=lax.Precision.HIGHEST,
        preferred_element_type=jnp.float32,
    )
    return (result[:, None], r_factor)


def solution(mesh):
    in_specs = (P("rows", "sub", None, None), P("rows", "sub"), P("rows", "sub"))
    out_specs = (P("rows", "sub", None, None), P())
    return jax.shard_map(
        per_device, mesh=mesh, in_specs=in_specs, out_specs=out_specs, check_vma=False
    )
```

profile of v0, /device:TPU:0, one launch (start us, length us, event | category | flops | bytes accessed | tf_op | source)
XLA Modules:
  0.0 661.5 jit_solution(13611043332102278474)
XLA Ops:
  10.8 7.3 %all-to-all-start = ((f32[8,8,1]{1,2,0:T(1,128)}), f32[8,8,1]{1,2,0:T(1,128)S(1)}, u32[]{:S(2)}, u32[]{:S(2)}) async-start(f32[8,8,1]{1,2,0:T(1,128)} %bitcast.5), calls=%async_computation | async-start | bytes 8192 | tf_op jit(solution)/shard_map/all_to_all | solution.py:72
  18.1 4.2 broadcast_in_dim.26
  22.3 16.0 %scatter_fusion = f32[64,128,256]{2,1,0:T(8,128)} fusion(f32[64,128,256]{2,1,0:T(8,128)} %broadcast_in_dim.26, s32[64]{0:T(128)S(1)} %fusion.38, f32[64,128,256]{2,1,0:T(8,128)} %bitcast.102), kind=kCustom, calls=%fused_computation.1 | custom fusion | bytes 25166080 | tf_op jit(solution)/shard_map/scatter | solution.py:64
  38.4 5.8 all-to-all-start.1
  44.4 182.5 %all-to-all-done.1 = f32[64,128,256]{2,1,0:T(8,128)} async-done(((f32[64,128,256]{2,1,0:T(8,128)}), f32[64,128,256]{2,1,0:T(8,128)}, u32[]{:S(2)}, u32[]{:S(2)}) %all-to-all-start.1) | async-done | bytes 8388640 | tf_op jit(solution)/shard_map/all_to_all | solution.py:71
  226.9 2.5 broadcast_in_dim.11
  229.4 15.4 %scatter_fusion.1 = f32[32,128,256]{2,1,0:T(8,128)} fusion(f32[32,128,256]{2,1,0:T(8,128)} %broadcast_in_dim.11, s32[64]{0:T(128)S(1)} %fusion.37, f32[64,128,256]{2,1,0:T(8,128)} %all-to-all-done.1), kind=kCustom, calls=%fused_computation.2 | custom fusion | bytes 25166080 | tf_op jit(solution)/shard_map/scatter | solution.py:76
  244.8 10.9 %fusion = f32[256,256]{0,1:T(8,128)} fusion(f32[32,128,256]{2,1,0:T(8,128)} %scatter_fusion.1), kind=kOutput, calls=%fused_computation.9 | convolution fusion | flops 3221291008 | bytes 4456448 | tf_op jit(solution)/shard_map/dot_general | solution.py:18
  256.0 124.2 %all-reduce.4.cloned.1.call-done = f32[256,256]{0,1:T(8,128)} async-done(((f32[256,256]{0,1:T(8,128)}), f32[256,256]{0,1:T(8,128)}) %all-reduce.4.cloned.1.call-update) | async-done | bytes 262160 | tf_op jit(solution)/shard_map/psum | solution.py:36
  382.3 11.7 %cholesky.130 = f32[128,128]{1,0:T(8,128)S(1)} custom-call(f32[128,128]{1,0:T(8,128)S(1)} %cholesky.194), custom_call_target="Cholesky" | custom-call | tf_op jit(solution)/shard_map/jit(cholesky)/cholesky | solution.py:10
  394.0 9.8 %custom-call.13 = f32[1,128,128]{1,2,0:T(8,128)S(1)} custom-call(f32[1,128,128]{2,1,0:T(8,128)S(1)} %get-tuple-element.55), custom_call_target="InvertDiagBlocksLowerTriangular" | custom-call | tf_op jit(solution)/shard_map/jit(cholesky)/cholesky | solution.py:10
  404.4 11.7 %cholesky.147 = f32[128,128]{1,0:T(8,128)S(1)} custom-call(f32[128,128]{1,0:T(8,128)S(1)} %convolution_subtract_fusion.3), custom_call_target="Cholesky" | custom-call | tf_op jit(solution)/shard_map/jit(cholesky)/cholesky | solution.py:10
  418.3 4.1 while.4
  422.4 19.7 %custom-call.14 = f32[2,128,128]{1,2,0:T(8,128)S(1)} custom-call(f32[2,128,128]{2,1,0:T(8,128)S(1)} %get-tuple-element.18), custom_call_target="InvertDiagBlocksLowerTriangular" | custom-call | tf_op jit(solution)/shard_map/triangular_solve/custom-call.0 | solution.py:12
  443.0 5.5 fusion.1
  448.5 1.9 copy-done
  450.4 7.4 %convolution_multiply_fusion = f32[256,256]{0,1:T(8,128)} fusion(f32[4096,256]{1,0:T(8,128)S(1)} %fusion.1), kind=kOutput, calls=%fused_computation.7 | convolution fusion | flops 3221291008 | bytes 4456448 | tf_op jit(solution)/shard_map/dot_general | solution.py:18
  457.9 124.1 %all-reduce.6.cloned.1.call-done = f32[256,256]{0,1:T(8,128)} async-done(((f32[256,256]{0,1:T(8,128)}), f32[256,256]{0,1:T(8,128)}) %all-reduce.6.cloned.1.call-update) | async-done | bytes 262160 | tf_op jit(solution)/shard_map/psum | solution.py:36
  584.1 11.7 %cholesky.164 = f32[128,128]{1,0:T(8,128)S(1)} custom-call(f32[128,128]{1,0:T(8,128)S(1)} %cholesky.197), custom_call_target="Cholesky" | custom-call | tf_op jit(solution)/shard_map/jit(cholesky)/cholesky | solution.py:10
  595.9 10.2 %custom-call.15 = f32[1,128,128]{1,2,0:T(8,128)S(1)} custom-call(f32[1,128,128]{2,1,0:T(8,128)S(1)} %get-tuple-element.51), custom_call_target="InvertDiagBlocksLowerTriangular" | custom-call | tf_op jit(solution)/shard_map/jit(cholesky)/cholesky | solution.py:10
  606.6 11.7 %cholesky.181 = f32[128,128]{1,0:T(8,128)S(1)} custom-call(f32[128,128]{1,0:T(8,128)S(1)} %convolution_subtract_fusion.2), custom_call_target="Cholesky" | custom-call | tf_op jit(solution)/shard_map/jit(cholesky)/cholesky | solution.py:10
  622.1 3.9 while.5
  626.1 19.8 %custom-call.16 = f32[2,128,128]{1,2,0:T(8,128)S(1)} custom-call(f32[2,128,128]{2,1,0:T(8,128)S(1)} %get-tuple-element.19), custom_call_target="InvertDiagBlocksLowerTriangular" | custom-call | tf_op jit(solution)/shard_map/triangular_solve/custom-call.0 | solution.py:12
  646.8 7.7 %fusion.5 = f32[4096,256]{1,0:T(8,128)} fusion(f32[4096,256]{1,0:T(8,128)} %copy-done, f32[128,256]{1,0:T(8,128)S(1)} %fusion.26, f32[128,256]{1,0:T(8,128)S(1)} %fusion.21), kind=kOutput, calls=%fused_computation.18 | convolution fusion | flops 3221291008 | bytes 8650752 | tf_op jit(solution)/shard_map/dot_general | solution.py:30
  (61 shorter events, 21.7 us)
Async XLA Ops:
  10.8 27.6 %all-to-all-start = ((f32[8,8,1]{1,2,0:T(1,128)}), f32[8,8,1]{1,2,0:T(1,128)S(1)}, u32[]{:S(2)}, u32[]{:S(2)}) async-start(f32[8,8,1]{1,2,0:T(1,128)} %bitcast.5), calls=%async_computation | async-start | bytes 8192 | tf_op jit(solution)/shard_map/all_to_all | solution.py:72
  38.4 188.5 %all-to-all-start.1 = ((f32[64,128,256]{2,1,0:T(8,128)}), f32[64,128,256]{2,1,0:T(8,128)}, u32[]{:S(2)}, u32[]{:S(2)}) async-start(f32[64,128,256]{2,1,0:T(8,128)} %scatter_fusion), calls=%async_computation.1 | async-start | bytes 16777216 | tf_op jit(solution)/shard_map/all_to_all | solution.py:71
  44.2 335.9 %all-reduce.4.cloned.1.call-start = ((), (), s32[]{:S(2)}) async-start(), calls=%async_computation.2 | async-start | bytes 524288 | tf_op jit(solution)/shard_map/psum | solution.py:36
  255.7 326.3 %all-reduce.6.cloned.1.call-start = ((), (), s32[]{:S(2)}) async-start(), calls=%async_computation.3 | async-start | bytes 524288 | tf_op jit(solution)/shard_map/psum | solution.py:36
  448.5 1.9 copy-start
Sparse Core Ops, SparseCore 0:
  255.8 124.3 all-reduce.3
  458.0 123.9 all-reduce.5
where the time goes:
time: 669 us; the launch traced here: 662 us
  waiting for transfers between devices  431 us (64%)
  other arithmetic  112 us (17%)
  local copies, waits for them, and re-layouts  51.9 us (8%)
  matrix products  35.4 us (5%)
  between operations  17.8 us (3%)
  starting transfers between devices  13.4 us (2%)
    psum x2, waiting for transfers between devices, reduce_gram(): return lax.psum(partial_value, ('rows', 'sub'))  248 us
    all_to_all x1, waiting for transfers between devices, per_device(): lax.all_to_all(outgoing, 'rows', split_axis=0, concat_axis=0, tiled=True)  182 us
    another operation x13, other arithmetic, factor(): lower = jnp.linalg.cholesky(gram)  69 us
    another operation x5, other arithmetic, factor(): lax.linalg.triangular_solve(lower, identity, left_side=True, lower=True)  39.6 us
    dot_general x2, matrix products, gram_of(): lax.dot_general(flattened, flattened, (((0,), (0,)), ((), ())), precision...  18.3 us
    scatter x1, local copies, waits for them, and re-layouts, per_device(): outgoing = jnp.zeros((devices_rows * per_slot, block_rows, width), jnp.fl...  16 us
    scatter x1, local copies, waits for them, and re-layouts, per_device(): jnp.zeros((BLK_DEV, block_rows, width), jnp.float32).at[place]  15.4 us
  transfers between devices with their start and end apart: 4, of which 3 were waited for; matrix products, arithmetic and copies ran while one was open for 3% of the time, Pallas kernels for 0%

commit v1 on v0

--- a/solution.py
+++ b/solution.py
@@ -33,7 +33,7 @@
 
 
 def reduce_gram(partial_value):
-    return lax.psum(partial_value, ("rows", "sub"))
+    return lax.psum(lax.psum(partial_value, "sub"), "rows")
 
 
 def per_device(held, held_block, held_count):

time: 669 us -> 631 us (0.943)
  waiting for transfers between devices: 431 us -> 393 us
    psum x2 -> x4, waiting for transfers between devices: 248 us -> 210 us  [reduce_gram(): return lax.psum(lax.psum(partial_value, 'sub'), 'rows')]
  transfers between devices with their start and end apart: 4 -> 6, of which waited for: 3 -> 5; matrix products, arithmetic and copies ran while one was open for 3% -> 3% of each run, Pallas kernels for 0% -> 0%
where the time goes in v1:
time: 631 us; the launch traced here: 623 us
  waiting for transfers between devices  393 us (62%)
  other arithmetic  112 us (18%)
  local copies, waits for them, and re-layouts  51.9 us (8%)
  matrix products  35.2 us (6%)
  between operations  17.4 us (3%)
  starting transfers between devices  13.9 us (2%)
    psum x4, waiting for transfers between devices, reduce_gram(): return lax.psum(lax.psum(partial_value, 'sub'), 'rows')  210 us
    all_to_all x1, waiting for transfers between devices, per_device(): lax.all_to_all(outgoing, 'rows', split_axis=0, concat_axis=0, tiled=True)  182 us
    another operation x13, other arithmetic, factor(): lower = jnp.linalg.cholesky(gram)  68.6 us
    another operation x5, other arithmetic, factor(): lax.linalg.triangular_solve(lower, identity, left_side=True, lower=True)  39.4 us
    dot_general x2, matrix products, gram_of(): lax.dot_general(flattened, flattened, (((0,), (0,)), ((), ())), precision...  18.3 us
    scatter x1, local copies, waits for them, and re-layouts, per_device(): outgoing = jnp.zeros((devices_rows * per_slot, block_rows, width), jnp.fl...  16 us
    scatter x1, local copies, waits for them, and re-layouts, per_device(): jnp.zeros((BLK_DEV, block_rows, width), jnp.float32).at[place]  15.4 us
    dot_general x2, matrix products, apply_inverse(): jnp.dot(flattened, inverse.T, precision=lax.Precision.HIGHEST, preferred_...  13 us
  transfers between devices with their start and end apart: 6, of which 5 were waited for; matrix products, arithmetic and copies ran while one was open for 3% of the time, Pallas kernels for 0%

profile of v1, /device:TPU:0, one launch (start us, length us, event | category | flops | bytes accessed | tf_op | source)
XLA Modules:
  0.0 623.3 jit_solution(18007971331506997065)
XLA Ops:
  10.8 7.3 %all-to-all-start = ((f32[8,8,1]{1,2,0:T(1,128)}), f32[8,8,1]{1,2,0:T(1,128)S(1)}, u32[]{:S(2)}, u32[]{:S(2)}) async-start(f32[8,8,1]{1,2,0:T(1,128)} %bitcast.5), calls=%async_computation | async-start | bytes 8192 | tf_op jit(solution)/shard_map/all_to_all | solution.py:72
  18.1 4.2 broadcast_in_dim.26
  22.3 16.0 %scatter_fusion = f32[64,128,256]{2,1,0:T(8,128)} fusion(f32[64,128,256]{2,1,0:T(8,128)} %broadcast_in_dim.26, s32[64]{0:T(128)S(1)} %fusion.38, f32[64,128,256]{2,1,0:T(8,128)} %bitcast.102), kind=kCustom, calls=%fused_computation.1 | custom fusion | bytes 25166080 | tf_op jit(solution)/shard_map/scatter | solution.py:64
  38.4 5.8 all-to-all-start.1
  44.4 182.5 %all-to-all-done.1 = f32[64,128,256]{2,1,0:T(8,128)} async-done(((f32[64,128,256]{2,1,0:T(8,128)}), f32[64,128,256]{2,1,0:T(8,128)}, u32[]{:S(2)}, u32[]{:S(2)}) %all-to-all-start.1) | async-done | bytes 8388640 | tf_op jit(solution)/shard_map/all_to_all | solution.py:71
  229.4 15.4 %scatter_fusion.1 = f32[32,128,256]{2,1,0:T(8,128)} fusion(f32[32,128,256]{2,1,0:T(8,128)} %broadcast_in_dim.11, s32[64]{0:T(128)S(1)} %fusion.37, f32[64,128,256]{2,1,0:T(8,128)} %all-to-all-done.1), kind=kCustom, calls=%fused_computation.2 | custom fusion | bytes 25166080 | tf_op jit(solution)/shard_map/scatter | solution.py:76
  244.8 10.9 %fusion = f32[256,256]{0,1:T(8,128)} fusion(f32[32,128,256]{2,1,0:T(8,128)} %scatter_fusion.1), kind=kOutput, calls=%fused_computation.9 | convolution fusion | flops 3221291008 | bytes 4456448 | tf_op jit(solution)/shard_map/dot_general | solution.py:18
  255.8 31.4 %all-reduce.6.cloned.1.call-done = f32[256,256]{0,1:T(8,128)} async-done(((f32[256,256]{0,1:T(8,128)}), f32[256,256]{0,1:T(8,128)}) %all-reduce.6.cloned.1.call-update) | async-done | bytes 262160 | tf_op jit(solution)/shard_map/psum | solution.py:36
  287.4 74.0 %all-reduce.8.cloned.1.call-done = f32[256,256]{0,1:T(8,128)} async-done(((f32[256,256]{0,1:T(8,128)}), f32[256,256]{0,1:T(8,128)}) %all-reduce.8.cloned.1.call-update) | async-done | bytes 262160 | tf_op jit(solution)/shard_map/psum | solution.py:36
  363.5 11.7 %cholesky.130 = f32[128,128]{1,0:T(8,128)S(1)} custom-call(f32[128,128]{1,0:T(8,128)S(1)} %cholesky.194), custom_call_target="Cholesky" | custom-call | tf_op jit(solution)/shard_map/jit(cholesky)/cholesky | solution.py:10
  375.2 9.8 %custom-call.13 = f32[1,128,128]{1,2,0:T(8,128)S(1)} custom-call(f32[1,128,128]{2,1,0:T(8,128)S(1)} %get-tuple-element.55), custom_call_target="InvertDiagBlocksLowerTriangular" | custom-call | tf_op jit(solution)/shard_map/jit(cholesky)/cholesky | solution.py:10
  385.6 11.7 %cholesky.147 = f32[128,128]{1,0:T(8,128)S(1)} custom-call(f32[128,128]{1,0:T(8,128)S(1)} %convolution_subtract_fusion.3), custom_call_target="Cholesky" | custom-call | tf_op jit(solution)/shard_map/jit(cholesky)/cholesky | solution.py:10
  399.4 4.3 while.4
  403.7 19.7 %custom-call.14 = f32[2,128,128]{1,2,0:T(8,128)S(1)} custom-call(f32[2,128,128]{2,1,0:T(8,128)S(1)} %get-tuple-element.18), custom_call_target="InvertDiagBlocksLowerTriangular" | custom-call | tf_op jit(solution)/shard_map/triangular_solve/custom-call.0 | solution.py:12
  424.3 5.3 fusion.1
  431.5 7.4 %convolution_multiply_fusion = f32[256,256]{0,1:T(8,128)} fusion(f32[4096,256]{1,0:T(8,128)S(1)} %fusion.1), kind=kOutput, calls=%fused_computation.7 | convolution fusion | flops 3221291008 | bytes 4456448 | tf_op jit(solution)/shard_map/dot_general | solution.py:18
  439.4 30.9 %all-reduce.10.cloned.1.call-done = f32[256,256]{0,1:T(8,128)} async-done(((f32[256,256]{0,1:T(8,128)}), f32[256,256]{0,1:T(8,128)}) %all-reduce.10.cloned.1.call-update) | async-done | bytes 262160 | tf_op jit(solution)/shard_map/psum | solution.py:36
  470.4 74.1 %all-reduce.12.cloned.1.call-done = f32[256,256]{0,1:T(8,128)} async-done(((f32[256,256]{0,1:T(8,128)}), f32[256,256]{0,1:T(8,128)}) %all-reduce.12.cloned.1.call-update) | async-done | bytes 262160 | tf_op jit(solution)/shard_map/psum | solution.py:36
  546.6 11.7 %cholesky.164 = f32[128,128]{1,0:T(8,128)S(1)} custom-call(f32[128,128]{1,0:T(8,128)S(1)} %cholesky.197), custom_call_target="Cholesky" | custom-call | tf_op jit(solution)/shard_map/jit(cholesky)/cholesky | solution.py:10
  558.4 9.8 %custom-call.15 = f32[1,128,128]{1,2,0:T(8,128)S(1)} custom-call(f32[1,128,128]{2,1,0:T(8,128)S(1)} %get-tuple-element.51), custom_call_target="InvertDiagBlocksLowerTriangular" | custom-call | tf_op jit(solution)/shard_map/jit(cholesky)/cholesky | solution.py:10
  568.7 11.7 %cholesky.181 = f32[128,128]{1,0:T(8,128)S(1)} custom-call(f32[128,128]{1,0:T(8,128)S(1)} %convolution_subtract_fusion.2), custom_call_target="Cholesky" | custom-call | tf_op jit(solution)/shard_map/jit(cholesky)/cholesky | solution.py:10
  584.2 4.1 while.5
  588.4 19.7 %custom-call.16 = f32[2,128,128]{1,2,0:T(8,128)S(1)} custom-call(f32[2,128,128]{2,1,0:T(8,128)S(1)} %get-tuple-element.19), custom_call_target="InvertDiagBlocksLowerTriangular" | custom-call | tf_op jit(solution)/shard_map/triangular_solve/custom-call.0 | solution.py:12
  609.0 7.7 %fusion.5 = f32[4096,256]{1,0:T(8,128)} fusion(f32[4096,256]{1,0:T(8,128)} %copy-done, f32[128,256]{1,0:T(8,128)S(1)} %fusion.26, f32[128,256]{1,0:T(8,128)S(1)} %fusion.21), kind=kOutput, calls=%fused_computation.18 | convolution fusion | flops 3221291008 | bytes 8650752 | tf_op jit(solution)/shard_map/dot_general | solution.py:30
  (67 shorter events, 26.6 us)
Async XLA Ops:
  10.8 27.6 %all-to-all-start = ((f32[8,8,1]{1,2,0:T(1,128)}), f32[8,8,1]{1,2,0:T(1,128)S(1)}, u32[]{:S(2)}, u32[]{:S(2)}) async-start(f32[8,8,1]{1,2,0:T(1,128)} %bitcast.5), calls=%async_computation | async-start | bytes 8192 | tf_op jit(solution)/shard_map/all_to_all | solution.py:72
  38.4 188.5 %all-to-all-start.1 = ((f32[64,128,256]{2,1,0:T(8,128)}), f32[64,128,256]{2,1,0:T(8,128)}, u32[]{:S(2)}, u32[]{:S(2)}) async-start(f32[64,128,256]{2,1,0:T(8,128)} %scatter_fusion), calls=%async_computation.1 | async-start | bytes 16777216 | tf_op jit(solution)/shard_map/all_to_all | solution.py:71
  44.2 242.9 %all-reduce.6.cloned.1.call-start = ((), (), s32[]{:S(2)}) async-start(), calls=%async_computation.2 | async-start | bytes 524288 | tf_op jit(solution)/shard_map/psum | solution.py:36
  255.7 105.7 %all-reduce.8.cloned.1.call-start = ((), (), s32[]{:S(2)}) async-start(), calls=%async_computation.3 | async-start | bytes 524288 | tf_op jit(solution)/shard_map/psum | solution.py:36
  287.1 183.2 %all-reduce.10.cloned.1.call-start = ((), (), s32[]{:S(2)}) async-start(), calls=%async_computation.4 | async-start | bytes 524288 | tf_op jit(solution)/shard_map/psum | solution.py:36
  429.6 1.9 copy-start
  439.0 105.5 %all-reduce.12.cloned.1.call-start = ((), (), s32[]{:S(2)}) async-start(), calls=%async_computation.5 | async-start | bytes 524288 | tf_op jit(solution)/shard_map/psum | solution.py:36
Sparse Core Ops, SparseCore 0:
  255.8 31.2 all-reduce.5
  290.8 70.5 all-reduce.7
  439.1 31.2 all-reduce.9
  473.9 70.5 all-reduce.11
